TPU v7x, 32 devices: a whole 2x2x4 slice. The times are simulated.
32 devices in a mesh: sec: 4 (over y, x), dev: 8 (over z, core).
Axes of the slice: x: 2, y: 2, z: 4, core: 2. Of those that a mesh axis runs over, the one named last changes fastest.
Arguments:
- strain_rows: bfloat16 [65536, 128], P(('sec', 'dev')), may hold values from -6 to 6
- bands: int32 [65536], P(('sec', 'dev')), may hold values from 0 to 15
- damaged: int32 [4096], P(('sec', 'dev')), may hold values from 0 to 2047
- owner: int32 [4096, 1], P(('sec', 'dev')), may hold values from 0 to 31; in each aligned block of 128 rows (0 to 127, 128 to 255, ...) at most 8 rows name the same one
- first_layers: bfloat16 [4096, 4096], P(('sec', 'dev')), may hold values from -0.5 to 0.5
- middle_weight: bfloat16 [4096, 4096], P(None, 'sec'), may hold values from -0.09375 to 0.09375
- out_weight: bfloat16 [4096, 128], P('sec'), may hold values from -0.09375 to 0.09375
- band_scale: float32 [16, 4096], replicated, may hold values from 0.5 to 2
- back_weight: bfloat16 [128, 128], replicated, may hold values from -0.5 to 0.5
Outputs:
- response: bfloat16 [4096, 128], P(('sec', 'dev'))
Inputs may be any that keep to these rules, and one draw needn't show every extreme that they name: Among the 128 rows of one macro device no owner is named more than 8 times, a bound that some block reaches. `damaged`: indices into the listing device's own 2048 points.
All inputs are finite; a program needn't handle non-finite values.
Results may differ from a plain program's by a relative error of at most 0.014.
Values may be sent and summed in bfloat16 or wider, within the bound.
No kernel may reach another device: no remote copies, remote signals or barrier semaphores. Data moves between devices by JAX's collectives and lax.ppermute only.
A program may use at most 128 MiB of HBM per device.

v0:
```python
import jax
import jax.numpy as jnp
from jax import lax
from jax.sharding import PartitionSpec as P

PASSES = 2


def scale_parts(band_scale):
    hi = band_scale.astype(jnp.bfloat16)
    rest = band_scale - hi.astype(jnp.float32)
    mid = rest.astype(jnp.bfloat16)
    lo = (rest - mid.astype(jnp.float32)).astype(jnp.bfloat16)
    return jnp.concatenate([hi, mid, lo], axis=0)


def band_rows(band_values, parts):
    levels = parts.shape[0] // 3
    level_ids = jnp.arange(3 * levels, dtype=jnp.int32) % levels
    picks = (band_values[:, None] == level_ids[None, :]).astype(jnp.bfloat16)
    return jnp.dot(picks, parts, preferred_element_type=jnp.float32)


def first_hidden(rows, weights, band_values, parts):
    mixed = jnp.einsum("srf,sfh->srh", rows, weights, preferred_element_type=jnp.float32)
    mixed = mixed.reshape(-1, weights.shape[2]) * band_rows(band_values, parts)
    return jax.nn.silu(mixed).astype(jnp.bfloat16)


def surrogate_tail(hidden_block, middle_weight, out_weight):
    middle = jax.nn.silu(
        jnp.dot(hidden_block, middle_weight, preferred_element_type=jnp.float32)
    ).astype(jnp.bfloat16)
    return jnp.dot(middle, out_weight, preferred_element_type=jnp.float32)


def per_device(
    strain_rows,
    bands,
    damaged,
    owner,
    first_layers,
    middle_weight,
    out_weight,
    band_scale,
    back_weight,
):
    n_sec = lax.axis_size("sec")
    n_dev = lax.axis_size("dev")
    count_all = n_sec * n_dev
    list_rows = damaged.shape[0]
    slot_count = max(2, 2 * list_rows // count_all)
    group_slots = n_sec * slot_count
    feat_width = strain_rows.shape[1]
    hid = first_layers.shape[1]
    every_first = lax.all_gather(first_layers, "sec", axis=0, tiled=True).reshape(
        n_sec, feat_width, hid
    )
    parts = scale_parts(band_scale)
    features = jnp.take(strain_rows, damaged, axis=0)
    band_local = jnp.take(bands, damaged)
    target_owner = owner[:, 0]
    matches = (target_owner[:, None] == jnp.arange(count_all, dtype=jnp.int32)[None, :]).astype(
        jnp.int32
    )
    slot_rank = jnp.sum((jnp.cumsum(matches, axis=0) - 1) * matches, axis=1)
    owner_sec = target_owner // n_dev
    owner_dev = target_owner % n_dev
    target = owner_dev * group_slots + owner_sec * slot_count + slot_rank
    dispatch = (
        jnp.arange(n_dev * group_slots, dtype=jnp.int32)[:, None] == target[None, :]
    ).astype(jnp.bfloat16)
    packed = jnp.concatenate([features, band_local.astype(jnp.bfloat16)[:, None]], axis=1)
    send = jnp.dot(dispatch, packed, preferred_element_type=jnp.float32).astype(jnp.bfloat16)
    send = send.reshape(1, n_dev, group_slots, feat_width + 1)
    send = jnp.broadcast_to(send, (n_sec, n_dev, group_slots, feat_width + 1)).reshape(
        count_all, group_slots, feat_width + 1
    )
    got = lax.all_to_all(send, ("sec", "dev"), split_axis=0, concat_axis=0, tiled=True)
    got = got.reshape(count_all, n_sec, slot_count, feat_width + 1).transpose(1, 0, 2, 3)
    got = got.reshape(n_sec, count_all * slot_count, feat_width + 1)
    rows = got[:, :, :feat_width]
    got_band = got[:, :, feat_width].astype(jnp.int32).reshape(-1)
    result = None
    for segment_index in range(PASSES):
        hidden = first_hidden(rows, every_first, got_band, parts)
        partial = surrogate_tail(hidden, middle_weight, out_weight)
        if segment_index + 1 < PASSES:
            values = lax.psum(partial, "sec").astype(jnp.bfloat16)
            rows = (
                rows.astype(jnp.float32)
                + jnp.dot(values, back_weight, preferred_element_type=jnp.float32).reshape(
                    rows.shape
                )
            ).astype(jnp.bfloat16)
        else:
            out_width = partial.shape[1]
            back = partial.reshape(n_sec, count_all, slot_count, out_width).transpose(1, 0, 2, 3)
            back = lax.all_to_all(back, ("sec", "dev"), split_axis=0, concat_axis=0, tiled=True)
            back = back.reshape(n_sec, n_dev * group_slots, out_width).sum(axis=0)
            result = jnp.take(back, target, axis=0).astype(jnp.bfloat16)
    return result


def solution(mesh):
    in_specs = (
        P(("sec", "dev"), None),
        P(("sec", "dev")),
        P(("sec", "dev")),
        P(("sec", "dev"), None),
        P(("sec", "dev"), None),
        P(None, "sec"),
        P("sec", None),
        P(),
        P(),
    )
    out_specs = P(("sec", "dev"), None)
    return jax.shard_map(
        per_device, mesh=mesh, in_specs=in_specs, out_specs=out_specs, check_vma=False
    )
```

profile of v0, /device:TPU:0, one launch (start us, length us, event | category | flops | bytes accessed | tf_op | source)
XLA Modules:
  0.0 186.2 jit_solution(1819267888237272443)
XLA Ops:
  6.5 0.7 all-gather.2.cloned.1.call-update
  7.9 1.6 gather_fusion.1
  9.6 0.7 gather_fusion
  10.3 0.7 convert_bitcast_fusion
  11.1 0.7 fusion.22
  12.0 0.8 select_reduce_fusion
  12.8 0.7 fusion.28
  13.9 0.8 broadcast_in_dim.47
  14.8 7.3 %all-to-all-start = ((bf16[32,32,129]{2,1,0:T(8,128)(2,1)}), bf16[32,32,129]{2,1,0:T(8,128)(2,1)S(1)}, u32[]{:S(2)}, u32[]{:S(2)}) async-start(bf16[32,32,129]{2,1,0:T(8,128)(2,1)} %bitcast.5), calls=%async_computation | async-start | bytes 1048576 | tf_op jit(solution)/shard_map/all_to_all | solution.py:79
  22.1 1.1 fusion.33
  23.2 15.2 %all-to-all-done = bf16[32,32,129]{2,1,0:T(8,128)(2,1)S(1)} async-done(((bf16[32,32,129]{2,1,0:T(8,128)(2,1)}), bf16[32,32,129]{2,1,0:T(8,128)(2,1)S(1)}, u32[]{:S(2)}, u32[]{:S(2)}) %all-to-all-start) | async-done | bytes 264224 | tf_op jit(solution)/shard_map/all_to_all | solution.py:79
  38.7 31.4 %all-gather.2.cloned.1.call-done = bf16[512,4096]{1,0:T(8,128)(2,1)} async-done(((bf16[128,4096]{1,0:T(8,128)(2,1)}), bf16[512,4096]{1,0:T(8,128)(2,1)}) %all-gather.2.cloned.1.call-update) | async-done | bytes 4194320 | tf_op jit(solution)/shard_map/all_gather | solution.py:56
  70.1 4.5 %fusion.14 = f32[4,256,4096]{2,1,0:T(8,128)S(1)} fusion(bf16[4,128,4096]{2,1,0:T(8,128)(2,1)} %bitcast.48, bf16[4,256,129]{2,1,0:T(8,128)(2,1)S(1)} %copy_bitcast_fusion.1), kind=kOutput, calls=%fused_computation.30 | convolution fusion | flops 1073741824 | bytes 21233664 | tf_op jit(solution)/shard_map/srf,sfh->srh/dot_general | solution.py:25
  74.7 10.1 %multiply_convert_fusion.1 = (bf16[1024,4096]{1,0:T(8,128)(2,1)}, f32[1024,4096]{1,0:T(8,128)}) fusion(f32[4,256,4096]{2,1,0:T(8,128)S(1)} %fusion.14, bf16[16,4096]{1,0:T(8,128)(2,1)S(1)} %get-tuple-element.10, bf16[16,4096]{1,0:T(8,128)(2,1)S(1)} %get-tuple-element.11, bf16[16,4096]{1,0:T(8,128)(2,1)S(1)} %get-tuple-element.9, s32[48]{0:T(128)S(1)} %and_select_fusion, ...), kind=kOutput, calls=%fused_computation.6 | convolution fusion | flops 429047808 | bytes 42340544 | tf_op jit(solution)/shard_map/dot_general | solution.py:21
  84.8 14.5 %fusion = f32[1024,128]{1,0:T(8,128)S(1)} fusion(bf16[1024,128]{1,0:T(8,128)(2,1)S(1)} %copy-done.4, bf16[1024,4096]{1,0:T(8,128)(2,1)} %get-tuple-element.12, bf16[4096,1024]{1,0:T(8,128)(2,1)} %param.14), kind=kOutput, calls=%fused_computation.9 | convolution fusion | flops 8863612928 | bytes 17563648 | tf_op jit(solution)/shard_map/dot_general | solution.py:34
  99.3 27.1 %all-reduce.1 = bf16[1024,128]{1,0:T(8,128)(2,1)S(1)} all-reduce(f32[1024,128]{1,0:T(8,128)S(1)} %fusion), channel_id=1, replica_groups=mesh['sec'=4,'dev'=8] {'sec'}, use_global_device_ids=true, to_apply=%region_2.3 | all-reduce | flops 131072 | bytes 786432 | tf_op jit(solution)/shard_map/psum | solution.py:89
  126.6 4.5 %fusion.9 = f32[4,256,4096]{2,1,0:T(8,128)S(1)} fusion(bf16[4,128,4096]{2,1,0:T(8,128)(2,1)} %bitcast.49, f32[4,256,128]{2,1,0:T(8,128)S(1)} %bitcast.50, bf16[4,256,129]{2,1,0:T(8,128)(2,1)S(1)} %copy_bitcast_fusion.1), kind=kOutput, calls=%fused_computation.23 | convolution fusion | flops 1074135040 | bytes 21757952 | tf_op jit(solution)/shard_map/srf,sfh->srh/dot_general | solution.py:25
  131.1 10.9 %multiply_convert_fusion = bf16[1024,4096]{1,0:T(8,128)(2,1)} fusion(f32[1024,4096]{1,0:T(8,128)} %get-tuple-element.13, f32[4,256,4096]{2,1,0:T(8,128)S(1)} %fusion.9), kind=kLoop, calls=%fused_computation.5 | loop fusion | flops 25165824 | bytes 41943040 | tf_op jit(solution)/shard_map/convert_element_type | solution.py:27
  142.0 14.5 %fusion.1 = f32[1024,128]{1,0:T(8,128)S(1)} fusion(bf16[1024,128]{1,0:T(8,128)(2,1)S(1)} %copy-done.4, bf16[1024,4096]{1,0:T(8,128)(2,1)} %multiply_convert_fusion, bf16[4096,1024]{1,0:T(8,128)(2,1)} %param.14), kind=kOutput, calls=%fused_computation.10 | convolution fusion | flops 8863612928 | bytes 17563648 | tf_op jit(solution)/shard_map/dot_general | solution.py:34
  156.6 0.8 copy.19
  157.4 4.2 %all-to-all-start.1 = ((f32[32,4,8,128]{3,2,1,0:T(8,128)}), f32[32,4,8,128]{3,2,1,0:T(8,128)S(1)}, u32[]{:S(2)}, u32[]{:S(2)}) async-start(f32[32,4,8,128]{3,2,1,0:T(8,128)} %bitcast.47), calls=%async_computation.1 | async-start | bytes 1048576 | tf_op jit(solution)/shard_map/all_to_all | solution.py:99
  161.7 16.2 %all-to-all-done.1 = f32[32,4,8,128]{3,2,1,0:T(8,128)S(1)} async-done(((f32[32,4,8,128]{3,2,1,0:T(8,128)}), f32[32,4,8,128]{3,2,1,0:T(8,128)S(1)}, u32[]{:S(2)}, u32[]{:S(2)}) %all-to-all-start.1) | async-done | bytes 524320 | tf_op jit(solution)/shard_map/all_to_all | solution.py:99
  178.0 0.7 gather_fusion.2
  178.7 0.7 select_convert_fusion
  (26 shorter events, 1.9 us)
Async XLA Ops:
  6.5 3.0 %copy-start = (bf16[2048,128]{1,0:T(8,128)(2,1)S(1)}, bf16[2048,128]{1,0:T(8,128)(2,1)}, u32[]{:S(2)}) copy-start(bf16[2048,128]{1,0:T(8,128)(2,1)} %param.9) | copy-start | bytes 1572868
  6.5 63.6 %all-gather.2.cloned.1.call-start = ((), (), s32[]{:S(2)}) async-start(), calls=%async_computation.2 | async-start | bytes 5242880 | tf_op jit(solution)/shard_map/all_gather | solution.py:56
  14.8 23.7 %all-to-all-start = ((bf16[32,32,129]{2,1,0:T(8,128)(2,1)}), bf16[32,32,129]{2,1,0:T(8,128)(2,1)S(1)}, u32[]{:S(2)}, u32[]{:S(2)}) async-start(bf16[32,32,129]{2,1,0:T(8,128)(2,1)} %bitcast.5), calls=%async_computation | async-start | bytes 1048576 | tf_op jit(solution)/shard_map/all_to_all | solution.py:79
  74.6 10.1 %copy-start.4 = (bf16[1024,128]{1,0:T(8,128)(2,1)S(1)}, bf16[1024,128]{1,0:T(8,128)(2,1)}, u32[]{:S(2)}) copy-start(bf16[1024,128]{1,0:T(8,128)(2,1)} %param.15) | copy-start | bytes 786436
  84.8 41.6 %copy-start.2 = (bf16[128,128]{1,0:T(8,128)(2,1)S(1)}, bf16[128,128]{1,0:T(8,128)(2,1)}, u32[]{:S(2)}) copy-start(bf16[128,128]{1,0:T(8,128)(2,1)} %param.17) | copy-start | bytes 98308
  142.0 19.7 %copy-start.3 = (s32[128,1]{0,1:T(1,128)S(1)}, s32[128,1]{0,1:T(1,128)}, u32[]{:S(2)}) copy-start(s32[128,1]{0,1:T(1,128)} %param.12) | copy-start | bytes 1540
  142.0 37.3 %copy-start.1 = (bf16[2048,128]{1,0:T(8,128)(2,1)S(1)}, bf16[2048,128]{1,0:T(8,128)(2,1)}, u32[]{:S(2)}) copy-start(bf16[2048,128]{1,0:T(8,128)(2,1)} %param.9) | copy-start | bytes 1572868
  157.4 20.5 %all-to-all-start.1 = ((f32[32,4,8,128]{3,2,1,0:T(8,128)}), f32[32,4,8,128]{3,2,1,0:T(8,128)S(1)}, u32[]{:S(2)}, u32[]{:S(2)}) async-start(f32[32,4,8,128]{3,2,1,0:T(8,128)} %bitcast.47), calls=%async_computation.1 | async-start | bytes 1048576 | tf_op jit(solution)/shard_map/all_to_all | solution.py:99
Sparse Core Ops, SparseCore 0:
  9.2 60.9 all-gather.1
where the time goes:
time: 187 us; the launch traced here: 186 us
  waiting for transfers between devices  63.6 us (34%)
  matrix products  48.6 us (26%)
  blocking collectives  27.1 us (14%)
  other arithmetic  16.8 us (9%)
  between operations  13.5 us (7%)
  starting transfers between devices  11.6 us (6%)
  local copies, waits for them, and re-layouts  5.03 us (3%)
    all_gather x1, waiting for transfers between devices, per_device(): lax.all_gather(first_layers, 'sec', axis=0, tiled=True)  31.4 us
    dot_general x2, matrix products, surrogate_tail(): return jnp.dot(middle, out_weight, preferred_element_type=jnp.float32)  29.1 us
    psum x1, blocking collectives, per_device(): values = lax.psum(partial, 'sec').astype(jnp.bfloat16)  27.1 us
    all_to_all x1, waiting for transfers between devices, per_device(): lax.all_to_all(back, ('sec', 'dev'), split_axis=0, concat_axis=0, tiled=T...  16.2 us
    all_to_all x1, waiting for transfers between devices, per_device(): lax.all_to_all(send, ('sec', 'dev'), split_axis=0, concat_axis=0, tiled=T...  15.2 us
    convert_element_type x1, other arithmetic, first_hidden(): return jax.nn.silu(mixed).astype(jnp.bfloat16)  10.9 us
    dot_general x1, matrix products, band_rows(): return jnp.dot(picks, parts, preferred_element_type=jnp.float32)  10.1 us
    dot_general x2, matrix products, first_hidden(): jnp.einsum('srf,sfh->srh', rows, weights, preferred_element_type=jnp.floa...  9.05 us
  transfers between devices with their start and end apart: 3, of which 3 were waited for; matrix products, arithmetic and copies ran while one was open for 5% of the time, Pallas kernels for 0%

commit v1 on v0

--- a/solution.py
+++ b/solution.py
@@ -86,7 +86,7 @@
         hidden = first_hidden(rows, every_first, got_band, parts)
         partial = surrogate_tail(hidden, middle_weight, out_weight)
         if segment_index + 1 < PASSES:
-            values = lax.psum(partial, "sec").astype(jnp.bfloat16)
+            values = jnp.sum(lax.all_gather(partial, "sec"), axis=0).astype(jnp.bfloat16)
             rows = (
                 rows.astype(jnp.float32)
                 + jnp.dot(values, back_weight, preferred_element_type=jnp.float32).reshape(

time: 187 us -> 199 us (1.064)
  waiting for transfers between devices: 63.6 us -> 98.9 us
  blocking collectives: 27.1 us -> 0 us
    all_gather x0 -> x1, waiting for transfers between devices: none -> 35.3 us  [per_device(): lax.all_gather(partial, 'sec')]
    psum x1 -> x0, blocking collectives: 27.1 us -> none  [per_device(): values = lax.psum(partial, 'sec').astype(jnp.bfloat16)]
  transfers between devices with their start and end apart: 3 -> 4, of which waited for: 3 -> 4; matrix products, arithmetic and copies ran while one was open for 5% -> 4% of each run, Pallas kernels for 0% -> 0%
where the time goes in v1:
time: 199 us
  waiting for transfers between devices  98.9 us (50%)
  matrix products  50.4 us (25%)
  other arithmetic  18.7 us (9%)
  between operations  13.5 us (7%)
  starting transfers between devices  12 us (6%)
  local copies, waits for them, and re-layouts  5.07 us (3%)
    all_gather x1, waiting for transfers between devices, per_device(): lax.all_gather(partial, 'sec')  35.3 us
    all_gather x1, waiting for transfers between devices, per_device(): lax.all_gather(first_layers, 'sec', axis=0, tiled=True)  31.4 us
    dot_general x2, matrix products, surrogate_tail(): return jnp.dot(middle, out_weight, preferred_element_type=jnp.float32)  30.6 us
    all_to_all x1, waiting for transfers between devices, per_device(): lax.all_to_all(back, ('sec', 'dev'), split_axis=0, concat_axis=0, tiled=T...  16.2 us
    all_to_all x1, waiting for transfers between devices, per_device(): lax.all_to_all(send, ('sec', 'dev'), split_axis=0, concat_axis=0, tiled=T...  15.2 us
    convert_element_type x1, other arithmetic, first_hidden(): return jax.nn.silu(mixed).astype(jnp.bfloat16)  11.1 us
    dot_general x1, matrix products, band_rows(): return jnp.dot(picks, parts, preferred_element_type=jnp.float32)  10.3 us
    dot_general x2, matrix products, first_hidden(): jnp.einsum('srf,sfh->srh', rows, weights, preferred_element_type=jnp.floa...  9.05 us
  transfers between devices with their start and end apart: 4, of which 4 were waited for; matrix products, arithmetic and copies ran while one was open for 4% of the time, Pallas kernels for 0%

profile of v1, /device:TPU:0, one launch (start us, length us, event | category | flops | bytes accessed | tf_op | source)
XLA Modules:
  0.0 198.5 jit_solution(3957255384183786157)
XLA Ops:
  6.5 0.7 all-gather.4.cloned.1.call-update
  7.9 1.6 gather_fusion.1
  9.6 0.7 gather_fusion
  11.1 0.7 fusion.22
  12.0 0.8 select_reduce_fusion
  12.8 0.7 fusion.28
  13.9 0.9 broadcast_in_dim.47
  14.8 7.3 %all-to-all-start = ((bf16[32,32,129]{2,1,0:T(8,128)(2,1)}), bf16[32,32,129]{2,1,0:T(8,128)(2,1)S(1)}, u32[]{:S(2)}, u32[]{:S(2)}) async-start(bf16[32,32,129]{2,1,0:T(8,128)(2,1)} %bitcast.5), calls=%async_computation | async-start | bytes 1048576 | tf_op jit(solution)/shard_map/all_to_all | solution.py:79
  22.2 1.1 fusion.33
  23.2 15.2 %all-to-all-done = bf16[32,32,129]{2,1,0:T(8,128)(2,1)S(1)} async-done(((bf16[32,32,129]{2,1,0:T(8,128)(2,1)}), bf16[32,32,129]{2,1,0:T(8,128)(2,1)S(1)}, u32[]{:S(2)}, u32[]{:S(2)}) %all-to-all-start) | async-done | bytes 264224 | tf_op jit(solution)/shard_map/all_to_all | solution.py:79
  38.7 31.4 %all-gather.4.cloned.1.call-done = bf16[512,4096]{1,0:T(8,128)(2,1)} async-done(((bf16[128,4096]{1,0:T(8,128)(2,1)}), bf16[512,4096]{1,0:T(8,128)(2,1)}) %all-gather.4.cloned.1.call-update) | async-done | bytes 4194320 | tf_op jit(solution)/shard_map/all_gather | solution.py:56
  70.1 4.5 %fusion.14 = f32[4,256,4096]{2,1,0:T(8,128)S(1)} fusion(bf16[4,128,4096]{2,1,0:T(8,128)(2,1)} %bitcast.49, bf16[4,256,129]{2,1,0:T(8,128)(2,1)S(1)} %copy_bitcast_fusion.1), kind=kOutput, calls=%fused_computation.30 | convolution fusion | flops 1073741824 | bytes 21233664 | tf_op jit(solution)/shard_map/srf,sfh->srh/dot_general | solution.py:25
  74.7 10.3 %multiply_convert_fusion.1 = (bf16[1024,4096]{1,0:T(8,128)(2,1)}, f32[1024,4096]{1,0:T(8,128)}) fusion(f32[4,256,4096]{2,1,0:T(8,128)S(1)} %fusion.14, bf16[16,4096]{1,0:T(8,128)(2,1)S(1)} %get-tuple-element.10, bf16[16,4096]{1,0:T(8,128)(2,1)S(1)} %get-tuple-element.11, bf16[16,4096]{1,0:T(8,128)(2,1)S(1)} %get-tuple-element.9, s32[48]{0:T(128)S(1)} %and_select_fusion, ...), kind=kOutput, calls=%fused_computation.6 | convolution fusion | flops 429047808 | bytes 42340544 | tf_op jit(solution)/shard_map/dot_general | solution.py:21
  84.9 16.1 %fusion = f32[1024,128]{1,0:T(8,128)} fusion(bf16[1024,128]{1,0:T(8,128)(2,1)S(1)} %copy-done.4, bf16[1024,4096]{1,0:T(8,128)(2,1)} %get-tuple-element.12, bf16[4096,1024]{1,0:T(8,128)(2,1)} %param.14), kind=kOutput, calls=%fused_computation.9 | convolution fusion | flops 8863612928 | bytes 17563648 | tf_op jit(solution)/shard_map/dot_general | solution.py:34
  101.0 35.3 %all-gather.6.cloned.1.call-done = f32[4096,128]{1,0:T(8,128)} async-done(((f32[1024,128]{1,0:T(8,128)}), f32[4096,128]{1,0:T(8,128)}) %all-gather.6.cloned.1.call-update) | async-done | bytes 2097168 | tf_op jit(solution)/shard_map/all_gather | solution.py:89
  136.4 1.7 reduce_sum.31
  138.3 4.5 %fusion.9 = f32[4,256,4096]{2,1,0:T(8,128)S(1)} fusion(bf16[4,128,4096]{2,1,0:T(8,128)(2,1)} %bitcast.50, f32[4,256,128]{2,1,0:T(8,128)S(1)} %bitcast.52, bf16[4,256,129]{2,1,0:T(8,128)(2,1)S(1)} %copy_bitcast_fusion.1), kind=kOutput, calls=%fused_computation.23 | convolution fusion | flops 1074135040 | bytes 21757952 | tf_op jit(solution)/shard_map/srf,sfh->srh/dot_general | solution.py:25
  142.9 11.1 %multiply_convert_fusion = bf16[1024,4096]{1,0:T(8,128)(2,1)} fusion(f32[1024,4096]{1,0:T(8,128)} %get-tuple-element.13, f32[4,256,4096]{2,1,0:T(8,128)S(1)} %fusion.9), kind=kLoop, calls=%fused_computation.5 | loop fusion | flops 25165824 | bytes 41943040 | tf_op jit(solution)/shard_map/convert_element_type | solution.py:27
  154.0 14.5 %fusion.1 = f32[1024,128]{1,0:T(8,128)S(1)} fusion(bf16[1024,128]{1,0:T(8,128)(2,1)S(1)} %copy-done.4, bf16[1024,4096]{1,0:T(8,128)(2,1)} %multiply_convert_fusion, bf16[4096,1024]{1,0:T(8,128)(2,1)} %param.14), kind=kOutput, calls=%fused_computation.10 | convolution fusion | flops 8863612928 | bytes 17563648 | tf_op jit(solution)/shard_map/dot_general | solution.py:34
  168.5 0.9 copy.19
  169.4 4.6 %all-to-all-start.1 = ((f32[32,4,8,128]{3,2,1,0:T(8,128)}), f32[32,4,8,128]{3,2,1,0:T(8,128)S(1)}, u32[]{:S(2)}, u32[]{:S(2)}) async-start(f32[32,4,8,128]{3,2,1,0:T(8,128)} %bitcast.48), calls=%async_computation.1 | async-start | bytes 1048576 | tf_op jit(solution)/shard_map/all_to_all | solution.py:99
  174.1 16.2 %all-to-all-done.1 = f32[32,4,8,128]{3,2,1,0:T(8,128)S(1)} async-done(((f32[32,4,8,128]{3,2,1,0:T(8,128)}), f32[32,4,8,128]{3,2,1,0:T(8,128)S(1)}, u32[]{:S(2)}, u32[]{:S(2)}) %all-to-all-start.1) | async-done | bytes 524320 | tf_op jit(solution)/shard_map/all_to_all | solution.py:99
  190.3 0.7 gather_fusion.2
  191.0 0.7 select_convert_fusion
  (29 shorter events, 2.6 us)
Async XLA Ops:
  6.5 3.0 %copy-start = (bf16[2048,128]{1,0:T(8,128)(2,1)S(1)}, bf16[2048,128]{1,0:T(8,128)(2,1)}, u32[]{:S(2)}) copy-start(bf16[2048,128]{1,0:T(8,128)(2,1)} %param.9) | copy-start | bytes 1572868
  6.5 63.6 %all-gather.4.cloned.1.call-start = ((), (), s32[]{:S(2)}) async-start(), calls=%async_computation.2 | async-start | bytes 5242880 | tf_op jit(solution)/shard_map/all_gather | solution.py:56
  14.8 23.7 %all-to-all-start = ((bf16[32,32,129]{2,1,0:T(8,128)(2,1)}), bf16[32,32,129]{2,1,0:T(8,128)(2,1)S(1)}, u32[]{:S(2)}, u32[]{:S(2)}) async-start(bf16[32,32,129]{2,1,0:T(8,128)(2,1)} %bitcast.5), calls=%async_computation | async-start | bytes 1048576 | tf_op jit(solution)/shard_map/all_to_all | solution.py:79
  22.1 114.3 %all-gather.6.cloned.1.call-start = ((), (), s32[]{:S(2)}) async-start(), calls=%async_computation.3 | async-start | bytes 2621440 | tf_op jit(solution)/shard_map/all_gather | solution.py:89
  74.6 10.3 %copy-start.4 = (bf16[1024,128]{1,0:T(8,128)(2,1)S(1)}, bf16[1024,128]{1,0:T(8,128)(2,1)}, u32[]{:S(2)}) copy-start(bf16[1024,128]{1,0:T(8,128)(2,1)} %param.15) | copy-start | bytes 786436
  84.9 53.2 %copy-start.2 = (bf16[128,128]{1,0:T(8,128)(2,1)S(1)}, bf16[128,128]{1,0:T(8,128)(2,1)}, u32[]{:S(2)}) copy-start(bf16[128,128]{1,0:T(8,128)(2,1)} %param.17) | copy-start | bytes 98308
  154.0 20.0 %copy-start.3 = (s32[128,1]{0,1:T(1,128)S(1)}, s32[128,1]{0,1:T(1,128)}, u32[]{:S(2)}) copy-start(s32[128,1]{0,1:T(1,128)} %param.12) | copy-start | bytes 1540
  154.0 37.7 %copy-start.1 = (bf16[2048,128]{1,0:T(8,128)(2,1)S(1)}, bf16[2048,128]{1,0:T(8,128)(2,1)}, u32[]{:S(2)}) copy-start(bf16[2048,128]{1,0:T(8,128)(2,1)} %param.9) | copy-start | bytes 1572868
  169.4 20.8 %all-to-all-start.1 = ((f32[32,4,8,128]{3,2,1,0:T(8,128)}), f32[32,4,8,128]{3,2,1,0:T(8,128)S(1)}, u32[]{:S(2)}, u32[]{:S(2)}) async-start(f32[32,4,8,128]{3,2,1,0:T(8,128)} %bitcast.48), calls=%async_computation.1 | async-start | bytes 1048576 | tf_op jit(solution)/shard_map/all_to_all | solution.py:99
Sparse Core Ops, SparseCore 0:
  9.2 60.9 all-gather.3
  101.2 35.1 all-gather.5
